TPU v7x, 128 devices: a whole 4x4x4 slice. The times are simulated.
128 devices in a mesh: row: 8 (over x_hi, z), col: 16 (over y, x_lo, core).
Axes of the slice: x: 4 (x_hi: 2, x_lo: 2; x = x_hi * 2 + x_lo), y: 4, z: 4, core: 2. Of those that a mesh axis runs over, the one named last changes fastest.
Arguments:
- residual: bfloat16 [1024, 16384], P('col', 'row'), may hold values from -16 to 16
- norm_gain: float32 [16384], P('row'), may hold values from 0.5 to 1.5
- query_weight: bfloat16 [16384, 16384], P('row', 'col'), may hold values from -0.046875 to 0.046875
- key_weight: bfloat16 [16384, 1024], P('row', 'col'), may hold values from -0.09375 to 0.09375
- value_weight: bfloat16 [16384, 1024], P('row', 'col'), may hold values from -0.25 to 0.25
- out_weight: bfloat16 [16384, 16384], P('col', 'row'), may hold values from -0.046875 to 0.046875
- kv_cache: bfloat16 [8, 2, 4096, 256], P(None, None, ('row', 'col')), may hold values from -72 to 72
- cache_lengths: int32 [2], replicated, may hold values from 1024 to 4096, as said below
Outputs:
- layer_out: bfloat16 [1024, 16384], P('col', 'row')
Inputs may be any that keep to these rules, and one draw needn't show every extreme that they name: `cache_lengths`: some sequence fills all 4096 slots.
All inputs are finite; a program needn't handle non-finite values.
Results may differ from a plain program's by a relative error of at most 0.019.
The roundings to bfloat16 on the way count: a program that leaves them out, or rounds other values in their place, can miss the bound.
Values may be sent and summed in bfloat16 or wider, within the bound.
No kernel may reach another device: no remote copies, remote signals or barrier semaphores. Data moves between devices by JAX's collectives and lax.ppermute only.
A program may use at most 64 MiB of HBM per device.

v0:
```python
import math

import jax
import jax.numpy as jnp
from jax import lax
from jax.sharding import PartitionSpec as P

D = 16384
KV_HEADS = 8
HEAD_DIM = 128
SEQS = 2
SPAN = 512
CACHE = 4096


ROPE_THETA = 500000.0
NORM_EPS = 1e-05


def partner_2(value, axis, bit):
    mask = 2**bit
    pairs = [(source, source ^ mask) for source in range(lax.axis_size(axis))]
    return lax.ppermute(value, axis, pairs)


def rotate(vectors, positions):
    half_dim = vectors.shape[-1] // 2
    frequency = jnp.power(
        ROPE_THETA, -2.0 * jnp.arange(half_dim, dtype=jnp.float32) / vectors.shape[-1]
    )
    angles = positions.astype(jnp.float32)[:, None] * frequency[None, :]
    cosine = jnp.cos(angles)[:, None, :]
    sine_part = jnp.sin(angles)[:, None, :]
    leading = vectors[..., :half_dim]
    second = vectors[..., half_dim:]
    return jnp.concatenate(
        [leading * cosine - second * sine_part, second * cosine + leading * sine_part], axis=-1
    )


def body(
    residual, norm_gain, query_weight, key_weight, value_weight, out_weight, kv_cache, cache_lengths
):
    row_devices = lax.axis_size("row")
    col_devices = lax.axis_size("col")
    row_index = lax.axis_index("row")
    col_index = lax.axis_index("col")
    tok_col = residual.shape[0]
    tok_row = tok_col * col_devices // row_devices
    query_cols = query_weight.shape[1]
    key_cols = key_weight.shape[1]
    heads_dev = query_cols // HEAD_DIM
    stream = residual.astype(jnp.float32)
    squares = lax.psum(jnp.sum(stream * stream, axis=1), "row")
    inverse_rms = lax.rsqrt(squares / D + NORM_EPS)
    normed_tile = (stream * inverse_rms[:, None] * norm_gain[None, :]).astype(jnp.bfloat16)
    normed = lax.all_gather(normed_tile, "col", axis=0, tiled=True)
    picked = normed
    summed = lax.psum_scatter(
        jnp.concatenate(
            [
                jnp.dot(picked, query_weight, preferred_element_type=jnp.float32),
                jnp.dot(picked, key_weight, preferred_element_type=jnp.float32),
                jnp.dot(picked, value_weight, preferred_element_type=jnp.float32),
            ],
            axis=1,
        ),
        "row",
        scatter_dimension=0,
        tiled=True,
    )
    first_row = row_index * tok_row
    sequence = first_row // SPAN
    offset = first_row % SPAN
    length = jnp.sum(jnp.where(jnp.arange(SEQS, dtype=jnp.int32) == sequence, cache_lengths, 0))
    positions = length + offset + jnp.arange(tok_row, dtype=jnp.int32)
    queries = rotate(
        summed[:, :query_cols].reshape(tok_row, heads_dev, HEAD_DIM), positions
    ).astype(jnp.bfloat16)
    new_pairs = summed[:, query_cols:].astype(jnp.bfloat16)
    head_pieces = new_pairs[:, None, :]
    bit_number = 0
    partner = partner_2(head_pieces, "col", bit_number)
    upper = col_index // (1 << bit_number) % 2 == 1
    head_pieces = jnp.where(
        upper,
        jnp.concatenate([partner, head_pieces], axis=1),
        jnp.concatenate([head_pieces, partner], axis=1),
    )
    own_keys = head_pieces[:, :, :key_cols].reshape(tok_row, HEAD_DIM)
    own_values = head_pieces[:, :, key_cols:].reshape(tok_row, HEAD_DIM)
    own_keys = rotate(own_keys.astype(jnp.float32)[:, None, :], positions)[:, 0, :].astype(
        jnp.bfloat16
    )
    pair_rows = jnp.concatenate([own_keys, own_values], axis=1)
    row_group = row_devices // SEQS
    for bit_number in range(row_group.bit_length() - 1):
        partner = partner_2(pair_rows, "row", bit_number)
        upper = row_index // (1 << bit_number) % 2 == 1
        pair_rows = jnp.where(
            upper,
            jnp.concatenate([partner, pair_rows], axis=0),
            jnp.concatenate([pair_rows, partner], axis=0),
        )
    slot_rows = jnp.repeat(kv_cache, col_devices // KV_HEADS, axis=0)
    spread = jnp.tile(slot_rows, (row_devices, 1, 1, 1))
    routed = lax.all_to_all(spread, ("row", "col"), split_axis=0, concat_axis=2, tiled=True)
    cache_rows = lax.dynamic_index_in_dim(routed[0], sequence, 0, keepdims=False)
    key_rows = jnp.concatenate([cache_rows[:, :HEAD_DIM], pair_rows[:, :HEAD_DIM]], axis=0)
    value_rows = jnp.concatenate([cache_rows[:, HEAD_DIM:], pair_rows[:, HEAD_DIM:]], axis=0)
    flat_query = jnp.transpose(queries, (1, 0, 2)).reshape(heads_dev * tok_row, HEAD_DIM)
    total_rows = heads_dev * tok_row
    block_rows = math.gcd(total_rows, 512)
    key_index = jnp.arange(CACHE + SPAN, dtype=jnp.int32)
    scale = 1.0 / math.sqrt(HEAD_DIM)

    def attend(block_index):
        begin_row = block_index * block_rows
        picked = lax.dynamic_slice_in_dim(flat_query, begin_row, block_rows, 0)
        query_pos = offset + (begin_row + jnp.arange(block_rows, dtype=jnp.int32)) % tok_row
        scores = (
            jnp.einsum("qd,kd->qk", picked, key_rows, preferred_element_type=jnp.float32) * scale
        )
        visible = jnp.where(
            key_index[None, :] < CACHE,
            (key_index < length)[None, :],
            key_index[None, :] - CACHE <= query_pos[:, None],
        )
        scores = jnp.where(visible, scores, -jnp.inf)
        row_max = jnp.max(scores, axis=1, keepdims=True)
        weights = jnp.exp(scores - row_max)
        totals = jnp.sum(weights, axis=1, keepdims=True)
        mixture = (
            jnp.dot(weights.astype(jnp.bfloat16), value_rows, preferred_element_type=jnp.float32)
            / totals
        )
        return mixture.astype(jnp.bfloat16)

    blocks = lax.map(attend, jnp.arange(total_rows // block_rows, dtype=jnp.int32))
    attended = jnp.transpose(blocks.reshape(heads_dev, tok_row, HEAD_DIM), (1, 0, 2)).reshape(
        tok_row, query_cols
    )
    head_rows = lax.all_gather(attended, "row", axis=0, tiled=True)
    picked = head_rows
    branch = lax.psum_scatter(
        jnp.dot(picked, out_weight, preferred_element_type=jnp.float32).astype(jnp.bfloat16),
        "col",
        scatter_dimension=0,
        tiled=True,
    ).astype(jnp.float32)
    return (residual.astype(jnp.float32) + branch).astype(jnp.bfloat16)


def solution(mesh):
    return jax.shard_map(
        body,
        mesh=mesh,
        in_specs=(
            P("col", "row"),
            P("row"),
            P("row", "col"),
            P("row", "col"),
            P("row", "col"),
            P("col", "row"),
            P(None, None, ("row", "col"), None),
            P(),
        ),
        out_specs=P("col", "row"),
        check_vma=False,
    )
```

profile of v0, /device:TPU:0, one launch (start us, length us, event | category | flops | bytes accessed | tf_op | source)
XLA Modules:
  0.0 391.0 jit_solution(2117644449863676531)
XLA Ops:
  7.7 25.6 %psum.7 = f32[64]{0:T(128)S(1)} all-reduce(f32[64]{0:T(128)S(1)} %fusion.23), channel_id=1, replica_groups=mesh['row'=8,'col'=16] {'row'}, use_global_device_ids=true, to_apply=%region_1.0 | all-reduce | flops 64 | bytes 512 | tf_op jit(solution)/shard_map/psum | solution.py:54
  33.3 1.8 fusion.25
  35.1 34.3 %all-gather.3.cloned.1.call-done = bf16[1024,2048]{1,0:T(8,128)(2,1)} async-done(((bf16[64,2048]{1,0:T(8,128)(2,1)}), bf16[1024,2048]{1,0:T(8,128)(2,1)}) %all-gather.3.cloned.1.call-update) | async-done | bytes 4194320 | tf_op jit(solution)/shard_map/all_gather | solution.py:57
  69.5 8.1 %fusion.41 = f32[1024,1024]{0,1:T(8,128)S(1)} fusion(bf16[1024,2048]{1,0:T(8,128)(2,1)} %all-gather.3.cloned.1.call-done, bf16[2048,1024]{1,0:T(8,128)(2,1)} %param.12), kind=kOutput, calls=%fused_computation.65 | convolution fusion | flops 4294967296 | bytes 12582912 | tf_op jit(solution)/shard_map/dot_general | solution.py:62
  80.4 2.5 pad_maximum_fusion
  83.9 2.6 tile.11
  86.5 9.2 %all-to-all-start = ((bf16[128,2,32,256]{3,2,1,0:T(8,128)(2,1)}), bf16[128,2,32,256]{3,2,1,0:T(8,128)(2,1)}, u32[]{:S(2)}, u32[]{:S(2)}) async-start(bf16[128,2,32,256]{3,2,1,0:T(8,128)(2,1)} %bitcast.49), calls=%async_computation.1 | async-start | bytes 8388608 | tf_op jit(solution)/shard_map/all_to_all | solution.py:107
  97.4 54.5 %all-to-all-done = bf16[128,2,32,256]{3,2,1,0:T(8,128)(2,1)} async-done(((bf16[128,2,32,256]{3,2,1,0:T(8,128)(2,1)}), bf16[128,2,32,256]{3,2,1,0:T(8,128)(2,1)}, u32[]{:S(2)}, u32[]{:S(2)}) %all-to-all-start) | async-done | bytes 4194336 | tf_op jit(solution)/shard_map/all_to_all | solution.py:107
  151.9 4.8 %copy.37 = bf16[128,2,32,256]{3,2,0,1:T(8,128)(2,1)} copy(bf16[128,2,32,256]{3,2,1,0:T(8,128)(2,1)} %all-to-all-done) | data formatting | bytes 8388608 | tf_op jit(solution)/shard_map/all_to_all | solution.py:107
  156.7 56.0 %reduce-scatter.3.cloned.1.call-done = f32[128,1152]{0,1:T(8,128)} async-done(((f32[1024,1152]{0,1:T(8,128)}), f32[128,1152]{0,1:T(8,128)}) %reduce-scatter.3.cloned.1.call-update) | async-done | bytes 589840 | tf_op jit(solution)/shard_map/reduce_scatter | solution.py:59
  213.5 1.8 dynamic-slice_bitcast_fusion
  217.1 3.1 collective-permute-done.1
  220.2 2.5 collective-permute-start.2
  223.7 3.4 collective-permute-done.2
  228.7 2.1 pad_maximum_fusion.1
  230.9 19.1 %while.14 = (s32[]{:T(128)}, bf16[2,512,128]{2,1,0:T(8,128)(2,1)}, s32[]{:T(128)}, s32[]{:T(128)}, s32[2]{0:T(128)S(1)}, /*index=5*/bf16[1024,128]{1,0:T(8,128)(...) while((s32[]{:T(128)}, bf16[2,512,128]{2,1,0:T(8,128)(2,1)}, ...), condition=%wide.region_7.8_spmd.clone.clone, body=%wide.region_4.7_spmd.clone.clone.sunk | while | flops 1229343744 | bytes 33100028 | solution.py:139
  232.9 3.9 %fusion.65 = (f32[512]{0:T(512)S(1)}, f32[512,4608]{1,0:T(8,128)S(1)}) fusion(bf16[4608,128]{1,0:T(8,128)(2,1)} %get-tuple-element.289, bf16[1024,128]{1,0:T(8,128)(2,1)} %get-tuple-element.288, s32[]{:T(128)S(6)} %select_n.134, s32[512]{0:T(512)S(1)} %fusion.64, s32[4608]{0:T(1024)S(1)} %iota_add_fusion.2, ...), kind=kOutput, calls=%fused_computation.61.clone.1 | convolution fusion | flops 615775744 | bytes 10779652 | tf_op jit(solution)/shard_map/while/body/eval_jaxpr/qd,kd->qk/dot_general | solution.py:122
  238.2 1.5 fusion.67
  242.4 3.9 %fusion.65 = (f32[512]{0:T(512)S(1)}, f32[512,4608]{1,0:T(8,128)S(1)}) fusion(bf16[4608,128]{1,0:T(8,128)(2,1)} %get-tuple-element.289, bf16[1024,128]{1,0:T(8,128)(2,1)} %get-tuple-element.288, s32[]{:T(128)S(6)} %select_n.134, s32[512]{0:T(512)S(1)} %fusion.64, s32[4608]{0:T(1024)S(1)} %iota_add_fusion.2, ...), kind=kOutput, calls=%fused_computation.61.clone.1 | convolution fusion | flops 615775744 | bytes 10779652 | tf_op jit(solution)/shard_map/while/body/eval_jaxpr/qd,kd->qk/dot_general | solution.py:122
  250.0 1.8 copy.40
  251.9 53.2 %all-gather.5.cloned.1.call-done = bf16[1024,1024]{0,1:T(8,128)(2,1)} async-done(((bf16[128,1024]{0,1:T(8,128)(2,1)}), bf16[1024,1024]{0,1:T(8,128)(2,1)}) %all-gather.5.cloned.1.call-update) | async-done | bytes 2097168 | tf_op jit(solution)/shard_map/all_gather | solution.py:143
  305.0 9.4 %convolution_convert_fusion = bf16[1024,2048]{1,0:T(8,128)(2,1)} fusion(bf16[1024,1024]{0,1:T(8,128)(2,1)} %all-gather.5.cloned.1.call-done, bf16[1024,2048]{1,0:T(8,128)(2,1)} %param.15), kind=kOutput, calls=%fused_computation.22 | convolution fusion | flops 4297064448 | bytes 10485760 | tf_op jit(solution)/shard_map/dot_general | solution.py:146
  314.4 68.3 %reduce-scatter.5.cloned.1.call-done = bf16[64,2048]{1,0:T(8,128)(2,1)} async-done(((bf16[1024,2048]{1,0:T(8,128)(2,1)}), bf16[64,2048]{1,0:T(8,128)(2,1)}) %reduce-scatter.5.cloned.1.call-update) | async-done | bytes 262160 | tf_op jit(solution)/shard_map/reduce_scatter | solution.py:145
  382.7 1.7 fusion.26
  (71 shorter events, 19.6 us)
Async XLA Ops:
  6.5 71.0 %copy-start = (bf16[2048,64]{0,1:T(8,128)(2,1)S(1)}, bf16[2048,64]{0,1:T(8,128)(2,1)}, u32[]{:S(2)}) copy-start(bf16[2048,64]{0,1:T(8,128)(2,1)} %param.13) | copy-start | bytes 786436
  6.5 62.9 %all-gather.3.cloned.1.call-start = ((), (), s32[]{:S(2)}) async-start(), calls=%async_computation.3 | async-start | bytes 4456448 | tf_op jit(solution)/shard_map/all_gather | solution.py:57
  35.1 177.6 %reduce-scatter.3.cloned.1.call-start = ((), (), s32[]{:S(2)}) async-start(), calls=%async_computation.4 | async-start | bytes 5308416 | tf_op jit(solution)/shard_map/reduce_scatter | solution.py:59
  69.5 8.1 %copy-start.1 = (bf16[1024,2048]{1,0:T(8,128)(2,1)S(1)}, bf16[1024,2048]{1,0:T(8,128)(2,1)}, u32[]{:S(2)}) copy-start(bf16[1024,2048]{1,0:T(8,128)(2,1)} %all-gather.3.cloned.1.call-done) | copy-start | bytes 12582916
  77.6 1.4 copy-start.3
  82.9 0.9 copy-start.4
  86.5 9.4 %copy-start.7 = (s32[2]{0:T(128)S(1)}, s32[2]{0:T(128)}, u32[]{:S(2)}) copy-start(s32[2]{0:T(128)} %param.17) | copy-start | bytes 28
  86.5 65.4 %all-to-all-start = ((bf16[128,2,32,256]{3,2,1,0:T(8,128)(2,1)}), bf16[128,2,32,256]{3,2,1,0:T(8,128)(2,1)}, u32[]{:S(2)}, u32[]{:S(2)}) async-start(bf16[128,2,32,256]{3,2,1,0:T(8,128)(2,1)} %bitcast.49), calls=%async_computation.1 | async-start | bytes 8388608 | tf_op jit(solution)/shard_map/all_to_all | solution.py:107
  95.7 209.3 %all-gather.5.cloned.1.call-start = ((), (), s32[]{:S(2)}) async-start(), calls=%async_computation.5 | async-start | bytes 2359296 | tf_op jit(solution)/shard_map/all_gather | solution.py:143
  213.5 1.8 collective-permute-start
  213.5 9.2 %slice-start = ((f32[128,1152]{0,1:T(8,128)}), f32[128,1024]{0,1:T(8,128)S(1)}, s32[]{:S(2)}) async-start(f32[128,1152]{0,1:T(8,128)} %reduce-scatter.3.cloned.1.call-done), calls=%async_computation.7 | async-start | bytes 1048576 | tf_op jit(solution)/shard_map/slice | solution.py:78
  215.6 4.6 %collective-permute-start.1 = (bf16[128,256]{0,1:T(8,128)(2,1)S(1)}, bf16[128,256]{0,1:T(8,128)(2,1)S(1)}, u32[]{:S(2)}, u32[]{:S(2)}) collective-permute-start(bf16[128,256]{0,1:T(8,128)(2,1)S(1)} %pad_maximum_fusion.3), channel_id=1, source_target_pairs={{0,16},{16,0},{32,48},{48,32},{64,80},{80,64},{96,112},{112,96},{1... | collective-permute-start | bytes 196616 | tf_op jit(solution)/shard_map/ppermute | solution.py:23
  220.2 6.8 %collective-permute-start.2 = (bf16[256,256]{0,1:T(8,128)(2,1)S(1)}, bf16[256,256]{0,1:T(8,128)(2,1)S(1)}, u32[]{:S(2)}, u32[]{:S(2)}) collective-permute-start(bf16[256,256]{0,1:T(8,128)(2,1)S(1)} %maximum_select_fusion.1), channel_id=1, source_target_pairs={{0,32},{16,48},{32,0},{48,16},{64,96},{80,112},{96,64},{112,80},{1... | collective-permute-start | bytes 393224 | tf_op jit(solution)/shard_map/ppermute | solution.py:23
  236.8 1.4 copy-start.5
  239.7 0.7 copy-start.6
  246.4 1.4 copy-start.5
  249.3 0.7 copy-start.6
  251.8 130.9 %reduce-scatter.5.cloned.1.call-start = ((), (), s32[]{:S(2)}) async-start(), calls=%async_computation.6 | async-start | bytes 4456448 | tf_op jit(solution)/shard_map/reduce_scatter | solution.py:145
  314.4 68.4 %copy-start.2 = (bf16[64,2048]{1,0:T(8,128)(2,1)S(1)}, bf16[64,2048]{1,0:T(8,128)(2,1)}, u32[]{:S(2)}) copy-start(bf16[64,2048]{1,0:T(8,128)(2,1)} %param.10) | copy-start | bytes 786436
Sparse Core Ops, SparseCore 0:
  35.2 34.2 all-gather.2
  83.0 129.5 reduce-scatter.2
  251.9 53.0 all-gather.4
  314.5 68.1 reduce-scatter.4
where the time goes:
time: 392 us; the launch traced here: 391 us
  waiting for transfers between devices  273 us (70%)
  matrix products  31.1 us (8%)
  blocking collectives  25.6 us (7%)
  local copies, waits for them, and re-layouts  18 us (5%)
  other arithmetic  14.8 us (4%)
  between operations  14.1 us (4%)
  starting transfers between devices  13.2 us (3%)
    reduce_scatter x1, waiting for transfers between devices, body(): lax.psum_scatter(jnp.dot(picked, out_weight, preferred_element_type=jnp.f...  68.3 us
    reduce_scatter x1, waiting for transfers between devices, body(): lax.psum_scatter(jnp.concatenate([jnp.dot(picked, query_weight, preferred...  56 us
    all_to_all x1, waiting for transfers between devices, body(): lax.all_to_all(spread, ('row', 'col'), split_axis=0, concat_axis=2, tiled...  54.5 us
    all_gather x1, waiting for transfers between devices, body(): head_rows = lax.all_gather(attended, 'row', axis=0, tiled=True)  53.2 us
    all_gather x1, waiting for transfers between devices, body(): normed = lax.all_gather(normed_tile, 'col', axis=0, tiled=True)  34.3 us
    psum x1, blocking collectives, body(): squares = lax.psum(jnp.sum(stream * stream, axis=1), 'row')  25.6 us
    dot_general x1, matrix products, body(): jnp.dot(picked, out_weight, preferred_element_type=jnp.float32)  9.36 us
    all_to_all x1, starting transfers between devices, body(): lax.all_to_all(spread, ('row', 'col'), split_axis=0, concat_axis=2, tiled...  9.21 us
  transfers between devices with their start and end apart: 8, of which 7 were waited for; matrix products, arithmetic and copies ran while one was open for 3% of the time, Pallas kernels for 0%

commit v1 on v0

--- a/solution.py
+++ b/solution.py
@@ -50,25 +50,32 @@
     query_cols = query_weight.shape[1]
     key_cols = key_weight.shape[1]
     heads_dev = query_cols // HEAD_DIM
+    group_cols = col_devices // KV_HEADS
+    group_rows = row_devices // SEQS
+    slots = kv_cache.shape[2]
+    by_seq = jnp.transpose(kv_cache, (1, 0, 2, 3))
+    send = jnp.repeat(jnp.repeat(by_seq, group_rows, axis=0), group_cols, axis=1)
+    send = send.reshape(row_devices * col_devices, slots, kv_cache.shape[3])
+    cache_rows = lax.all_to_all(send, ("row", "col"), 0, 0, tiled=True)
+    cache_rows = cache_rows.reshape(row_devices * col_devices * slots, kv_cache.shape[3])
+    gathered = lax.all_gather(residual, "col", axis=0, tiled=True)
     stream = residual.astype(jnp.float32)
     squares = lax.psum(jnp.sum(stream * stream, axis=1), "row")
     inverse_rms = lax.rsqrt(squares / D + NORM_EPS)
-    normed_tile = (stream * inverse_rms[:, None] * norm_gain[None, :]).astype(jnp.bfloat16)
-    normed = lax.all_gather(normed_tile, "col", axis=0, tiled=True)
-    picked = normed
-    summed = lax.psum_scatter(
-        jnp.concatenate(
-            [
-                jnp.dot(picked, query_weight, preferred_element_type=jnp.float32),
-                jnp.dot(picked, key_weight, preferred_element_type=jnp.float32),
-                jnp.dot(picked, value_weight, preferred_element_type=jnp.float32),
-            ],
-            axis=1,
-        ),
-        "row",
-        scatter_dimension=0,
-        tiled=True,
+    inverse_rms = lax.all_gather(inverse_rms, "col", axis=0, tiled=True)
+    normed = (gathered.astype(jnp.float32) * inverse_rms[:, None] * norm_gain[None, :]).astype(
+        jnp.bfloat16
     )
+    partial = jnp.concatenate(
+        [
+            jnp.dot(normed, query_weight, preferred_element_type=jnp.float32).astype(jnp.bfloat16),
+            jnp.dot(normed, key_weight, preferred_element_type=jnp.float32).astype(jnp.bfloat16),
+            jnp.dot(normed, value_weight, preferred_element_type=jnp.float32).astype(jnp.bfloat16),
+        ],
+        axis=1,
+    )
+    pieces = lax.all_to_all(partial, "row", 0, 0, tiled=True)
+    summed = pieces.reshape(row_devices, tok_row, -1).astype(jnp.float32).sum(axis=0)
     first_row = row_index * tok_row
     sequence = first_row // SPAN
     offset = first_row % SPAN
@@ -102,10 +109,6 @@
             jnp.concatenate([partner, pair_rows], axis=0),
             jnp.concatenate([pair_rows, partner], axis=0),
         )
-    slot_rows = jnp.repeat(kv_cache, col_devices // KV_HEADS, axis=0)
-    spread = jnp.tile(slot_rows, (row_devices, 1, 1, 1))
-    routed = lax.all_to_all(spread, ("row", "col"), split_axis=0, concat_axis=2, tiled=True)
-    cache_rows = lax.dynamic_index_in_dim(routed[0], sequence, 0, keepdims=False)
     key_rows = jnp.concatenate([cache_rows[:, :HEAD_DIM], pair_rows[:, :HEAD_DIM]], axis=0)
     value_rows = jnp.concatenate([cache_rows[:, HEAD_DIM:], pair_rows[:, HEAD_DIM:]], axis=0)
     flat_query = jnp.transpose(queries, (1, 0, 2)).reshape(heads_dev * tok_row, HEAD_DIM)
@@ -142,12 +145,9 @@
     )
     head_rows = lax.all_gather(attended, "row", axis=0, tiled=True)
     picked = head_rows
-    branch = lax.psum_scatter(
-        jnp.dot(picked, out_weight, preferred_element_type=jnp.float32).astype(jnp.bfloat16),
-        "col",
-        scatter_dimension=0,
-        tiled=True,
-    ).astype(jnp.float32)
+    products = jnp.dot(picked, out_weight, preferred_element_type=jnp.float32).astype(jnp.bfloat16)
+    products = lax.all_to_all(products, "col", 0, 0, tiled=True)
+    branch = products.reshape(col_devices, tok_col, -1).astype(jnp.float32).sum(axis=0)
     return (residual.astype(jnp.float32) + branch).astype(jnp.bfloat16)
 
 

time: 392 us -> 302 us (0.77)
  waiting for transfers between devices: 273 us -> 111 us
  blocking collectives: 25.6 us -> 107 us
  local copies, waits for them, and re-layouts: 18 us -> 12.6 us
    reduce_scatter x2 -> x0, waiting for transfers between devices: 124 us -> none  [the longest x1 68.3 us: body(): lax.psum_scatter(jnp.dot(picked, out_weight, preferred_element_type=jnp.f...]
    all_to_all x0 -> x1, blocking collectives: none -> 54.3 us  [body(): products = lax.all_to_all(products, 'col', 0, 0, tiled=True)]
    all_gather x1, waiting for transfers between devices: 34.3 us -> 0.02 us  [body(): gathered = lax.all_gather(residual, 'col', axis=0, tiled=True)]
    unnamed x0 -> x1, blocking collectives: none -> 27.2 us
    all_to_all x1 -> x0, local copies, waits for them, and re-layouts: 4.78 us -> none  [body(): lax.all_to_all(spread, ('row', 'col'), split_axis=0, concat_axis=2, tiled...]
    all_to_all x1 -> x2, waiting for transfers between devices: 54.5 us -> 53.8 us  [the longest x1 29.3 us: body(): pieces = lax.all_to_all(partial, 'row', 0, 0, tiled=True)]
    all_to_all x1 -> x2, starting transfers between devices: 9.21 us -> 9.54 us  [the longest x1 5.93 us: body(): cache_rows = lax.all_to_all(send, ('row', 'col'), 0, 0, tiled=True)]
  transfers between devices with their start and end apart: 8 -> 7, of which waited for: 7 -> 5; matrix products, arithmetic and copies ran while one was open for 3% -> 2% of each run, Pallas kernels for 0% -> 0%
where the time goes in v1:
time: 302 us; the launch traced here: 301 us
  waiting for transfers between devices  111 us (37%)
  blocking collectives  107 us (35%)
  matrix products  29.8 us (10%)
  between operations  15.1 us (5%)
  local copies, waits for them, and re-layouts  12.6 us (4%)
  other arithmetic  12.5 us (4%)
  starting transfers between devices  11 us (4%)
    all_to_all x1, blocking collectives, body(): products = lax.all_to_all(products, 'col', 0, 0, tiled=True)  54.3 us
    all_gather x1, waiting for transfers between devices, body(): head_rows = lax.all_gather(attended, 'row', axis=0, tiled=True)  50.5 us
    all_to_all x1, waiting for transfers between devices, body(): pieces = lax.all_to_all(partial, 'row', 0, 0, tiled=True)  29.3 us
    unnamed x1, blocking collectives  27.2 us
    psum x1, blocking collectives, body(): squares = lax.psum(jnp.sum(stream * stream, axis=1), 'row')  25.6 us
    all_to_all x1, waiting for transfers between devices, body(): cache_rows = lax.all_to_all(send, ('row', 'col'), 0, 0, tiled=True)  24.5 us
    dot_general x1, matrix products, body(): jnp.dot(normed, query_weight, preferred_element_type=jnp.float32)  8.53 us
    dot_general x2, matrix products, attend(): jnp.einsum('qd,kd->qk', picked, key_rows, preferred_element_type=jnp.floa...  7.86 us
  transfers between devices with their start and end apart: 7, of which 5 were waited for; matrix products, arithmetic and copies ran while one was open for 2% of the time, Pallas kernels for 0%

profile of v1, /device:TPU:0, one launch (start us, length us, event | category | flops | bytes accessed | tf_op | source)
XLA Modules:
  0.0 300.8 jit_solution(5329939803903337364)
XLA Ops:
  10.3 25.6 %psum.7 = f32[64]{0:T(128)S(1)} all-reduce(f32[64]{0:T(128)S(1)} %fusion.23), channel_id=1, replica_groups=mesh['row'=8,'col'=16] {'row'}, use_global_device_ids=true, to_apply=%region_1.0 | all-reduce | flops 64 | bytes 512 | tf_op jit(solution)/shard_map/psum | solution.py:63
  36.0 27.2 %all-reduce = f32[1024]{0:T(1024)S(1)} all-reduce(f32[1024]{0:T(1024)S(1)} %rsqrt_dynamic-update-slice_fusion), channel_id=1, replica_groups=mesh['row'=8,'col'=16] {'col'}, use_global_device_ids=true, to_apply=%add | all-reduce | flops 1024 | bytes 8192
  63.3 8.5 %convolution_convert_fusion.1 = bf16[1024,1024]{0,1:T(8,128)(2,1)S(1)} fusion(bf16[2048,1024]{1,0:T(8,128)(2,1)} %param.12, bf16[1024,2048]{1,0:T(8,128)(2,1)} %all-gather.3.cloned.1.call-done, f32[2048]{0:T(1024)} %param.11, f32[1024]{0:T(1024)S(1)} %all-reduce), kind=kOutput, calls=%fused_computation.27 | convolution fusion | flops 4304404480 | bytes 10498048 | tf_op jit(solution)/shard_map/dot_general | solution.py:71
  71.8 1.5 convolution_convert_fusion.2
  73.4 1.5 convolution_convert_fusion.3
  74.9 1.8 copy_bitcast_fusion
  76.7 3.6 %all-to-all-start = ((bf16[8,128,1152]{1,2,0:T(8,128)(2,1)}), bf16[8,128,1152]{1,2,0:T(8,128)(2,1)S(1)}, u32[]{:S(2)}, u32[]{:S(2)}) async-start(bf16[8,128,1152]{1,2,0:T(8,128)(2,1)} %copy_bitcast_fusion), calls=%async_computation | async-start | bytes 4718592 | tf_op jit(solution)/shard_map/all_to_all | solution.py:77
  80.4 29.3 %all-to-all-done = bf16[8,128,1152]{1,2,0:T(8,128)(2,1)S(1)} async-done(((bf16[8,128,1152]{1,2,0:T(8,128)(2,1)}), bf16[8,128,1152]{1,2,0:T(8,128)(2,1)S(1)}, u32[]{:S(2)}, u32[]{:S(2)}) %all-to-all-start) | async-done | bytes 2359328 | tf_op jit(solution)/shard_map/all_to_all | solution.py:77
  109.8 1.6 broadcast_in_dim.74
  111.4 5.9 %all-to-all-start.1 = ((bf16[128,32,256]{2,1,0:T(8,128)(2,1)}), bf16[128,32,256]{2,1,0:T(8,128)(2,1)}, u32[]{:S(2)}, u32[]{:S(2)}) async-start(bf16[128,32,256]{2,1,0:T(8,128)(2,1)} %bitcast.47), calls=%async_computation.1 | async-start | bytes 4194304 | tf_op jit(solution)/shard_map/all_to_all | solution.py:59
  122.8 24.5 %all-to-all-done.1 = bf16[128,32,256]{2,1,0:T(8,128)(2,1)} async-done(((bf16[128,32,256]{2,1,0:T(8,128)(2,1)}), bf16[128,32,256]{2,1,0:T(8,128)(2,1)}, u32[]{:S(2)}, u32[]{:S(2)}) %all-to-all-start.1) | async-done | bytes 2097184 | tf_op jit(solution)/shard_map/all_to_all | solution.py:59
  147.3 1.7 fusion.35
  150.3 5.5 %collective-permute-done.2 = bf16[256,256]{0,1:T(8,128)(2,1)S(1)} collective-permute-done((bf16[256,256]{0,1:T(8,128)(2,1)S(1)}, bf16[256,256]{0,1:T(8,128)(2,1)S(1)}, u32[]{:S(2)}, u32[]{:S(2)}) %collective-permute-start.2) | collective-permute-done | bytes 131104 | tf_op jit(solution)/shard_map/ppermute | solution.py:23
  157.4 2.1 pad_maximum_fusion
  159.6 18.7 %while.14 = (s32[]{:T(128)}, bf16[2,512,128]{2,1,0:T(8,128)(2,1)}, s32[]{:T(128)}, s32[]{:T(128)}, s32[2]{0:T(128)S(1)}, /*index=5*/bf16[1024,128]{1,0:T(8,128)(...) while((s32[]{:T(128)}, bf16[2,512,128]{2,1,0:T(8,128)(2,1)}, ...), condition=%wide.region_7.8_spmd.clone.clone, body=%wide.region_4.7_spmd.clone.clone.sunk | while | flops 1229343744 | bytes 33100028 | solution.py:142
  161.3 3.9 %fusion.56 = (f32[512]{0:T(512)S(1)}, f32[512,4608]{1,0:T(8,128)S(1)}) fusion(bf16[4608,128]{1,0:T(8,128)(2,1)} %get-tuple-element.289, bf16[1024,128]{1,0:T(8,128)(2,1)} %get-tuple-element.288, s32[]{:T(128)S(6)} %select_n.129, s32[512]{0:T(512)S(1)} %fusion.55, s32[4608]{0:T(1024)S(1)} %iota_add_fusion.2, ...), kind=kOutput, calls=%fused_computation.63.clone.1 | convolution fusion | flops 615775744 | bytes 10779652 | tf_op jit(solution)/shard_map/while/body/eval_jaxpr/qd,kd->qk/dot_general | solution.py:125
  165.3 1.4 fusion.57
  166.7 1.5 fusion.58
  170.7 3.9 %fusion.56 = (f32[512]{0:T(512)S(1)}, f32[512,4608]{1,0:T(8,128)S(1)}) fusion(bf16[4608,128]{1,0:T(8,128)(2,1)} %get-tuple-element.289, bf16[1024,128]{1,0:T(8,128)(2,1)} %get-tuple-element.288, s32[]{:T(128)S(6)} %select_n.129, s32[512]{0:T(512)S(1)} %fusion.55, s32[4608]{0:T(1024)S(1)} %iota_add_fusion.2, ...), kind=kOutput, calls=%fused_computation.63.clone.1 | convolution fusion | flops 615775744 | bytes 10779652 | tf_op jit(solution)/shard_map/while/body/eval_jaxpr/qd,kd->qk/dot_general | solution.py:125
  176.0 1.5 fusion.58
  178.2 1.8 copy.45
  180.0 50.5 %all-gather.5.cloned.1.call-done = bf16[1024,1024]{0,1:T(8,128)(2,1)} async-done(((bf16[128,1024]{0,1:T(8,128)(2,1)}), bf16[1024,1024]{0,1:T(8,128)(2,1)}) %all-gather.5.cloned.1.call-update) | async-done | bytes 2097168 | tf_op jit(solution)/shard_map/all_gather | solution.py:146
  230.6 7.4 %convolution_convert_fusion = bf16[1024,2048]{1,0:T(8,128)(2,1)S(1)} fusion(bf16[1024,1024]{0,1:T(8,128)(2,1)} %all-gather.5.cloned.1.call-done, bf16[1024,2048]{1,0:T(8,128)(2,1)} %param.15), kind=kOutput, calls=%fused_computation.24 | convolution fusion | flops 4297064448 | bytes 10485760 | tf_op jit(solution)/shard_map/dot_general | solution.py:148
  238.0 54.3 %all_to_all.23 = bf16[16,64,2048]{2,1,0:T(8,128)(2,1)S(1)} all-to-all(bf16[16,64,2048]{2,1,0:T(8,128)(2,1)S(1)} %bitcast.49), channel_id=1, replica_groups=mesh['row'=8,'col'=16] {'col'}, dimensions={0} | all-to-all | bytes 8388608 | tf_op jit(solution)/shard_map/all_to_all | solution.py:149
  (77 shorter events, 17.8 us)
Async XLA Ops:
  6.5 65.3 %copy-start = (bf16[2048,64]{0,1:T(8,128)(2,1)S(1)}, bf16[2048,64]{0,1:T(8,128)(2,1)}, u32[]{:S(2)}) copy-start(bf16[2048,64]{0,1:T(8,128)(2,1)} %param.14) | copy-start | bytes 786436
  6.5 56.7 %all-gather.3.cloned.1.call-start = ((), (), s32[]{:S(2)}) async-start(), calls=%async_computation.3 | async-start | bytes 4456448 | tf_op jit(solution)/shard_map/all_gather | solution.py:61
  63.2 8.6 %copy-start.8 = (f32[2048]{0:T(1024)S(1)}, f32[2048]{0:T(1024)}, u32[]{:S(2)}) copy-start(f32[2048]{0:T(1024)} %param.11) | copy-start | bytes 24580
  63.3 8.6 %copy-start.6 = (bf16[1024,2048]{1,0:T(8,128)(2,1)S(1)}, bf16[1024,2048]{1,0:T(8,128)(2,1)}, u32[]{:S(2)}) copy-start(bf16[1024,2048]{1,0:T(8,128)(2,1)} %all-gather.3.cloned.1.call-done) | copy-start | bytes 12582916
  71.8 1.5 copy-start.7
  74.9 5.5 %copy-start.3 = (bf16[8,2,32,256]{3,2,1,0:T(8,128)(2,1)S(1)}, bf16[8,2,32,256]{3,2,1,0:T(8,128)(2,1)}, u32[]{:S(2)}) copy-start(bf16[8,2,32,256]{3,2,1,0:T(8,128)(2,1)} %param.16) | copy-start | bytes 786436
  76.7 33.0 %all-to-all-start = ((bf16[8,128,1152]{1,2,0:T(8,128)(2,1)}), bf16[8,128,1152]{1,2,0:T(8,128)(2,1)S(1)}, u32[]{:S(2)}, u32[]{:S(2)}) async-start(bf16[8,128,1152]{1,2,0:T(8,128)(2,1)} %copy_bitcast_fusion), calls=%async_computation | async-start | bytes 4718592 | tf_op jit(solution)/shard_map/all_to_all | solution.py:77
  80.4 37.0 %copy-start.9 = (s32[2]{0:T(128)S(1)}, s32[2]{0:T(128)}, u32[]{:S(2)}) copy-start(s32[2]{0:T(128)} %param.17) | copy-start | bytes 28
  111.4 35.9 %all-to-all-start.1 = ((bf16[128,32,256]{2,1,0:T(8,128)(2,1)}), bf16[128,32,256]{2,1,0:T(8,128)(2,1)}, u32[]{:S(2)}, u32[]{:S(2)}) async-start(bf16[128,32,256]{2,1,0:T(8,128)(2,1)} %bitcast.47), calls=%async_computation.1 | async-start | bytes 4194304 | tf_op jit(solution)/shard_map/all_to_all | solution.py:59
  117.4 113.2 %all-gather.5.cloned.1.call-start = ((), (), s32[]{:S(2)}) async-start(), calls=%async_computation.4 | async-start | bytes 2359296 | tf_op jit(solution)/shard_map/all_gather | solution.py:146
  119.1 0.8 copy-start.2
  119.9 29.4 %slice-start = ((f32[128,1152]{0,1:T(8,128)}), f32[128,1024]{0,1:T(8,128)S(1)}, s32[]{:S(2)}) async-start(f32[128,1152]{0,1:T(8,128)} %copy-done.2), calls=%async_computation.5 | async-start | bytes 1048576 | tf_op jit(solution)/shard_map/slice | solution.py:85
  120.1 1.3 collective-permute-start
  121.7 27.3 %collective-permute-start.1 = (bf16[128,256]{0,1:T(8,128)(2,1)S(1)}, bf16[128,256]{0,1:T(8,128)(2,1)S(1)}, u32[]{:S(2)}, u32[]{:S(2)}) collective-permute-start(bf16[128,256]{0,1:T(8,128)(2,1)S(1)} %pad_maximum_fusion.2), channel_id=1, source_target_pairs={{0,16},{16,0},{32,48},{48,32},{64,80},{80,64},{96,112},{112,96},{1... | collective-permute-start | bytes 196616 | tf_op jit(solution)/shard_map/ppermute | solution.py:23
  149.0 6.7 %collective-permute-start.2 = (bf16[256,256]{0,1:T(8,128)(2,1)S(1)}, bf16[256,256]{0,1:T(8,128)(2,1)S(1)}, u32[]{:S(2)}, u32[]{:S(2)}) collective-permute-start(bf16[256,256]{0,1:T(8,128)(2,1)S(1)} %maximum_select_fusion.1), channel_id=1, source_target_pairs={{0,32},{16,48},{32,0},{48,16},{64,96},{80,112},{96,64},{112,80},{1... | collective-permute-start | bytes 393224 | tf_op jit(solution)/shard_map/ppermute | solution.py:23
  165.3 1.4 copy-start.4
  168.2 0.7 copy-start.5
  174.6 1.4 copy-start.4
  177.5 0.7 copy-start.5
  292.3 1.0 copy-start.1
Sparse Core Ops, SparseCore 0:
  9.0 39.6 all-gather.2
  180.1 50.3 all-gather.4
